TPU v7x, 128 devices: a whole 4x4x4 slice. The times are simulated.
128 devices in a mesh: wide: 64 (over z, y, x), narrow: 2 (over core).
Axes of the slice: x: 4, y: 4, z: 4, core: 2. Of those that a mesh axis runs over, the one named last changes fastest.
Arguments:
- tokens: bfloat16 [65536, 2048], P('wide', 'narrow'), may hold values from -6 to 6
- attn_gain: bfloat16 [2048], replicated, may hold values from 0.5 to 1.5
- q_weight: bfloat16 [2048, 3072], P('wide', 'narrow'), may hold values from -6 to 6
- kva_weight: bfloat16 [2048, 576], P('wide'), may hold values from -0.125 to 0.125
- kv_gain: bfloat16 [512], replicated, may hold values from 0.5 to 1.5
- kvb_weight: bfloat16 [512, 4096], P(None, 'narrow'), may hold values from -0.25 to 0.25
- o_weight: bfloat16 [2048, 2048], P('narrow'), may hold values from -0.125 to 0.125
- adapter_down: bfloat16 [2048, 1024], P(None, 'narrow'), may hold values from -0.125 to 0.125
- adapter_up_weight: bfloat16 [1024, 3072], P(None, 'narrow'), may hold values from -1.5 to 1.5
- lengths: int32 [64, 4], P('wide'), may hold values from 1 to 512, 1024 in all within a row
- adapter_ids: int32 [64, 4], P('wide'), may hold values from 0 to 63
- adapter_slot: int32 [64], replicated, may hold values from 0 to 63, each once
Outputs:
- hidden: bfloat16 [65536, 2048], P('wide', 'narrow')
- latent_cache: bfloat16 [65536, 576], P('wide')
Inputs may be any that keep to these rules, and one draw needn't show every extreme that they name: Each row of lengths sums to 1024, and its longest prompt is exactly 512.
All inputs are finite; a program needn't handle non-finite values.
Results may differ from a plain program's by a relative error of at most 0.0095.
The roundings to bfloat16 on the way count: a program that leaves them out, or rounds other values in their place, can miss the bound.
Values may be sent and summed in bfloat16 or wider, within the bound.
No kernel may reach another device: no remote copies, remote signals or barrier semaphores. Data moves between devices by JAX's collectives and lax.ppermute only.
A program may use at most 192 MiB of HBM per device.

v0:
```python
import jax
import jax.numpy as jnp
from jax import lax
from jax.sharding import PartitionSpec as P

NOPE = 128
ROPE = 64
VDIM = 128
LATENT = 512
RANK = 16
EPS = 1e-06
THETA = 50000.0
ADAPTER_SCALE = 2.0


def rms_scale(values, gain):
    mean_sq = jnp.mean(values * values, axis=-1, keepdims=True)
    return values * lax.rsqrt(mean_sq + EPS) * gain.astype(jnp.float32)


def rotate(values, positions):
    half = values.shape[-1] // 2
    freqs = jnp.exp(-jnp.log(THETA) * 2.0 * jnp.arange(half).astype(jnp.float32) / (2 * half))
    angle = positions.astype(jnp.float32)[:, None] * freqs[None, :]
    cosine = jnp.cos(angle)
    sine = jnp.sin(angle)
    if values.ndim == 3:
        cosine = cosine[:, None, :]
        sine = sine[:, None, :]
    first = values[..., :half]
    second = values[..., half:]
    return jnp.concatenate(
        [first * cosine - second * sine, first * sine + second * cosine], axis=-1
    )


def token_tables(length_row, id_row, adapter_slot, local_pos):
    ends = jnp.cumsum(length_row)
    starts = ends - length_row
    prompt = jnp.sum((ends[None, :] <= local_pos[:, None]).astype(jnp.int32), axis=1)
    onehot = (prompt[:, None] == jnp.arange(length_row.shape[0])[None, :]).astype(jnp.int32)
    position = local_pos - jnp.sum(onehot * starts[None, :], axis=1)
    adapter = jnp.sum(onehot * id_row[None, :], axis=1)
    slot_hot = (adapter[:, None] == jnp.arange(adapter_slot.shape[0])[None, :]).astype(jnp.int32)
    slot = jnp.sum(slot_hot * adapter_slot[None, :], axis=1)
    return (prompt, position, adapter, slot)


def pick_columns(stored, first_slots, prompts_here):
    blocks = [
        lax.dynamic_slice_in_dim(stored, first_slots[prompt_index] * RANK, RANK, 1)
        for prompt_index in range(prompts_here)
    ]
    return jnp.concatenate(blocks, axis=1)


def body(
    tokens,
    attn_gain,
    q_weight,
    kva_weight,
    kv_gain,
    kvb_weight,
    o_weight,
    adapter_down,
    adapter_up_weight,
    lengths,
    adapter_ids,
    adapter_slot,
):
    rows = tokens.shape[0]
    heads_here = o_weight.shape[0] // VDIM
    prompts_here = lengths.shape[1]
    whole = lax.all_gather(tokens, "narrow", axis=1, tiled=True)
    normed = rms_scale(whole.astype(jnp.float32), attn_gain).astype(jnp.bfloat16)
    local_pos = jnp.arange(rows)
    prompt, position, adapter, slot = token_tables(
        lengths[0], adapter_ids[0], adapter_slot, local_pos
    )
    query_vectors = jnp.dot(
        normed,
        lax.all_gather(q_weight, "wide", axis=0, tiled=True),
        preferred_element_type=jnp.float32,
    )
    kv_pre = jnp.dot(
        normed,
        lax.all_gather(kva_weight, "wide", axis=0, tiled=True),
        preferred_element_type=jnp.float32,
    )
    prompt_ids = adapter_ids[0]
    id_hot = (prompt_ids[:, None] == jnp.arange(adapter_slot.shape[0])[None, :]).astype(jnp.int32)
    prompt_position_slot = jnp.sum(id_hot * adapter_slot[None, :], axis=1)
    member = (prompt[:, None] == jnp.arange(prompts_here)[None, :]).astype(jnp.float32)
    stored = lax.all_gather(adapter_down, "narrow", axis=1, tiled=True)
    chosen = pick_columns(stored, prompt_position_slot, prompts_here)
    low = jnp.dot(normed, chosen, preferred_element_type=jnp.float32).reshape(
        rows, prompts_here, RANK
    )
    lowrank = jnp.sum(low * member[:, :, None], axis=1).astype(jnp.bfloat16)
    up_blocks = [
        lax.dynamic_slice_in_dim(adapter_up_weight, prompt_ids[prompt_index] * RANK, RANK, 0)
        for prompt_index in range(prompts_here)
    ]
    up_weight_rows = jnp.concatenate(up_blocks, axis=0)
    spread_rows = (member.astype(jnp.bfloat16)[:, :, None] * lowrank[:, None, :]).reshape(
        rows, prompts_here * RANK
    )
    query_vectors = query_vectors + ADAPTER_SCALE * jnp.dot(
        spread_rows, up_weight_rows, preferred_element_type=jnp.float32
    )
    query_vectors = query_vectors.reshape(rows, heads_here, NOPE + ROPE)
    query_vectors = jnp.concatenate(
        [query_vectors[..., :NOPE], rotate(query_vectors[..., NOPE:], position)], axis=-1
    ).astype(jnp.bfloat16)
    latent = rms_scale(kv_pre[:, :LATENT], kv_gain).astype(jnp.bfloat16)
    key_rope = rotate(kv_pre[:, LATENT:], position).astype(jnp.bfloat16)
    latent_cache = jnp.concatenate([latent, key_rope], axis=1)
    expanded = jnp.dot(latent, kvb_weight, preferred_element_type=jnp.float32).astype(jnp.bfloat16)
    expanded = expanded.reshape(rows, heads_here, NOPE + VDIM)
    key_nope = expanded[..., :NOPE]
    values = expanded[..., NOPE:]
    scale = 1.0 / jnp.sqrt(jnp.float32(NOPE + ROPE))
    scores = jnp.einsum(
        "qhd,khd->hqk", query_vectors[..., :NOPE], key_nope, preferred_element_type=jnp.float32
    )
    scores = scores + jnp.einsum(
        "qhd,kd->hqk", query_vectors[..., NOPE:], key_rope, preferred_element_type=jnp.float32
    )
    scores = scores * scale
    allowed = (prompt[None, :] == prompt[:, None]) & (local_pos[None, :] <= local_pos[:, None])
    scores = jnp.where(allowed[None, :, :], scores, jnp.float32(-1e30))
    top = jnp.max(scores, axis=-1, keepdims=True)
    expo = jnp.exp(scores - top)
    weights = (expo / jnp.sum(expo, axis=-1, keepdims=True)).astype(jnp.bfloat16)
    attended = jnp.einsum(
        "hqk,khd->qhd", weights, values, preferred_element_type=jnp.float32
    ).astype(jnp.bfloat16)
    attended = attended.reshape(rows, heads_here * VDIM)
    partial_out = jnp.dot(attended, o_weight, preferred_element_type=jnp.float32)
    projected = lax.psum_scatter(
        partial_out.astype(jnp.bfloat16), "narrow", scatter_dimension=1, tiled=True
    ).astype(jnp.float32)
    hidden = (tokens.astype(jnp.float32) + projected).astype(jnp.bfloat16)
    return (hidden, latent_cache)


def solution(mesh):
    return jax.shard_map(
        body,
        mesh=mesh,
        in_specs=(
            P("wide", "narrow"),
            P(),
            P("wide", "narrow"),
            P("wide", None),
            P(),
            P(None, "narrow"),
            P("narrow", None),
            P(None, "narrow"),
            P(None, "narrow"),
            P("wide", None),
            P("wide", None),
            P(),
        ),
        out_specs=(P("wide", "narrow"), P("wide", None)),
        check_vma=False,
    )
```

profile of v0, /device:TPU:1, one launch (start us, length us, event | category | flops | bytes accessed | tf_op | source)
XLA Modules:
  0.0 301.0 jit_solution(9721617435012271668)
XLA Ops:
  7.2 0.0 copy-start
  7.2 0.0 all-gather.5.cloned.1.call-start
  7.3 0.7 all-gather.5.cloned.1.call-update
  8.0 0.0 all-gather.11.cloned.1.call-start
  8.0 0.7 all-gather.11.cloned.1.call-update
  8.7 0.0 all-gather.7.cloned.1.call-start
  8.8 0.7 all-gather.7.cloned.1.call-update
  9.5 0.0 all-gather.9.cloned.1.call-start
  9.5 0.5 all-gather.9.cloned.1.call-update
  10.0 0.0 reduce-scatter.2.cloned.1.call-start
  10.1 0.2 select_reduce_fusion.1
  10.3 0.6 fusion.47
  13.5 0.7 fusion.46
  16.5 0.2 reduce-window.4
  16.8 0.5 multiply_exponential_fusion
  17.3 0.1 convert_reduce_fusion
  17.4 0.1 select_reduce_fusion
  17.5 1.6 constant_dynamic-slice_fusion.3
  19.1 0.6 fusion.7
  19.7 10.1 %all-gather.5.cloned.1.call-done = bf16[1024,2048]{1,0:T(8,128)(2,1)} async-done(((bf16[1024,1024]{1,0:T(8,128)(2,1)}), bf16[1024,2048]{1,0:T(8,128)(2,1)}) %all-gather.5.cloned.1.call-update) | async-done | bytes 4194320 | tf_op jit(solution)/shard_map/all_gather | solution.py:74
  29.8 3.1 %fusion.4 = f32[1024]{0:T(1024)S(1)} fusion(bf16[1024,2048]{1,0:T(8,128)(2,1)} %all-gather.5.cloned.1.call-done), kind=kLoop, calls=%fused_computation.9 | loop fusion | flops 6290432 | bytes 4198400 | tf_op jit(solution)/shard_map/reduce_sum | solution.py:17
  32.9 16.3 %all-gather.11.cloned.1.call-done = bf16[2048,1024]{1,0:T(8,128)(2,1)} async-done(((bf16[2048,512]{1,0:T(8,128)(2,1)}), bf16[2048,1024]{1,0:T(8,128)(2,1)}) %all-gather.11.cloned.1.call-update) | async-done | bytes 4194320 | tf_op jit(solution)/shard_map/all_gather | solution.py:94
  49.2 2.4 constant_dynamic-slice_fusion.7
  51.5 0.5 copy-done.2
  52.0 2.0 fusion.17
  54.2 64.3 %all-gather.7.cloned.1.call-done = bf16[2048,576]{1,0:T(8,128)(2,1)} async-done(((bf16[32,576]{1,0:T(8,128)(2,1)}), bf16[2048,576]{1,0:T(8,128)(2,1)}) %all-gather.7.cloned.1.call-update) | async-done | bytes 2359312 | tf_op jit(solution)/shard_map/all_gather | solution.py:87
  118.5 5.7 %fusion.43 = f32[1024,576]{0,1:T(8,128)S(1)} fusion(bf16[2048,576]{1,0:T(8,128)(2,1)} %all-gather.7.cloned.1.call-done, bf16[1024,2048]{1,0:T(8,128)(2,1)} %all-gather.5.cloned.1.call-done, f32[2048]{0:T(1024)S(1)} %convert_element_type.88, f32[1024]{0:T(1024)S(1)} %add_rsqrt_fusion.1), kind=kOutput, calls=%fused_computation.81 | convolution fusion | flops 2424307712 | bytes 8925184 | tf_op jit(solution)/shard_map/dot_general | solution.py:85
  124.2 0.2 multiply_reduce_fusion
  124.4 0.2 multiply_convert_fusion
  124.6 0.0 copy-start.3
  124.6 2.4 convolution_convert_fusion
  127.0 1.5 copy.40
  128.5 1.2 subtract_convert_fusion.1
  129.8 1.6 fusion.45
  131.4 60.1 %all-gather.9.cloned.1.call-done = bf16[2048,1536]{1,0:T(8,128)(2,1)} async-done(((bf16[32,1536]{1,0:T(8,128)(2,1)}), bf16[2048,1536]{1,0:T(8,128)(2,1)}) %all-gather.9.cloned.1.call-update) | async-done | bytes 6291472 | tf_op jit(solution)/shard_map/all_gather | solution.py:82
  191.4 10.1 %fusion.41 = f32[1024,1536]{1,0:T(8,128)S(1)} fusion(bf16[2048,1536]{1,0:T(8,128)(2,1)} %all-gather.9.cloned.1.call-done, bf16[1024,2048]{1,0:T(8,128)(2,1)} %all-gather.5.cloned.1.call-done, f32[2048]{0:T(1024)S(1)} %convert_element_type.88, f32[1024]{0:T(1024)S(1)} %add_rsqrt_fusion.1), kind=kOutput, calls=%fused_computation.80 | convolution fusion | flops 6450839552 | bytes 16789504 | tf_op jit(solution)/shard_map/dot_general | solution.py:80
  201.6 3.7 %multiply_add_fusion = f32[1024,1536]{1,0:T(8,128)} fusion(f32[1024,1536]{1,0:T(8,128)S(1)} %fusion.41, bf16[1024,64]{0,1:T(8,128)(2,1)S(1)} %bitcast.47, bf16[16,1536]{1,0:T(8,128)(2,1)S(1)} %copy-done.8, bf16[16,1536]{1,0:T(8,128)(2,1)S(1)} %copy-done.9, bf16[16,1536]{1,0:T(8,128)(2,1)S(1)} %copy-done.7, bf16[16,1536]{1,0:T(8,128)(2,1)S(1)} %copy-done.6), kind=kOutput, calls=%fused_computation.12 | convolution fusion | flops 205258752 | bytes 12910592 | tf_op jit(solution)/shard_map/dot_general | solution.py:108
  205.3 6.7 %copy.32 = f32[1024,1536]{0,1:T(8,128)} copy(f32[1024,1536]{1,0:T(8,128)} %multiply_add_fusion) | data formatting | bytes 12582912 | tf_op jit(solution)/shard_map/add | solution.py:108
  212.0 1.9 subtract_convert_fusion
  213.8 13.4 %fusion.13 = f32[1024,1024,8]{1,0,2:T(8,128)} fusion(bf16[1024,8,32]{0,2,1:T(8,128)(2,1)S(1)} %get-tuple-element.3, bf16[1024,8,32]{0,2,1:T(8,128)(2,1)S(1)} %get-tuple-element.2, bf16[1024,32]{0,1:T(8,128)(2,1)S(1)} %get-tuple-element.15, bf16[1024,32]{0,1:T(8,128)(2,1)S(1)} %get-tuple-element.14), kind=kOutput, calls=%fused_computation.25 | convolution fusion | flops 1076101120 | bytes 34734080 | tf_op jit(solution)/shard_map/qhd,kd->hqk/dot_general | solution.py:126
  227.2 26.8 %fusion.48 = (f32[8,1024]{1,0:T(8,128)S(1)}, f32[8,1024,1024]{1,2,0:T(8,128)}) fusion(f32[1024,1024,8]{1,0,2:T(8,128)} %fusion.13, pred[1024,1024]{0,1:T(8,128)(4,1)S(1)} %fusion.7, f32[1024,8,192]{0,2,1:T(8,128)} %bitcast.44, bf16[1024,8,128]{2,1,0:T(8,128)(2,1)S(1)} %get-tuple-element.5), kind=kOutput, calls=%fused_computation.85 | convolution fusion | flops 2189427712 | bytes 72384512 | tf_op jit(solution)/shard_map/sub | solution.py:133
  254.0 12.7 %fusion.10 = bf16[8,128,1024]{2,1,0:T(8,128)(2,1)S(1)} fusion(f32[8,1024,1024]{1,2,0:T(8,128)} %get-tuple-element.29, f32[8,1024]{1,0:T(8,128)S(1)} %get-tuple-element.28, bf16[1024,8,128]{2,1,0:T(8,128)(2,1)} %get-tuple-element.4), kind=kOutput, calls=%fused_computation.23 | convolution fusion | flops 2165309440 | bytes 37781504 | tf_op jit(solution)/shard_map/hqk,khd->qhd/dot_general | solution.py:135
  266.7 8.3 %convolution_convert_fusion.1 = bf16[1024,2048]{1,0:T(8,128)(2,1)} fusion(bf16[1024,1024]{0,1:T(8,128)(2,1)S(1)} %bitcast.52, bf16[1024,2048]{1,0:T(8,128)(2,1)} %param.18), kind=kOutput, calls=%fused_computation.18 | convolution fusion | flops 4297064448 | bytes 10485760 | tf_op jit(solution)/shard_map/dot_general | solution.py:139
  275.0 0.0 reduce-scatter.2.cloned.1.call-update
  275.1 1.2 copy-done.4
  276.3 1.1 pad_maximum_fusion
  277.4 12.6 %reduce-scatter.2.cloned.1.call-done = bf16[1024,1024]{1,0:T(8,128)(2,1)} async-done(((bf16[1024,2048]{1,0:T(8,128)(2,1)}), bf16[1024,1024]{1,0:T(8,128)(2,1)}) %reduce-scatter.2.cloned.1.call-update) | async-done | bytes 2097168 | tf_op jit(solution)/shard_map/reduce_scatter | solution.py:140
  289.9 4.5 %add_convert_fusion = bf16[1024,1024]{1,0:T(8,128)(2,1)} fusion(bf16[1024,1024]{1,0:T(8,128)(2,1)} %reduce-scatter.2.cloned.1.call-done, bf16[1024,1024]{1,0:T(8,128)(2,1)} %param.12), kind=kLoop, calls=%fused_computation.14 | loop fusion | flops 4194304 | bytes 6291456 | tf_op jit(solution)/shard_map/convert_element_type | solution.py:143
  (37 shorter events, 0.1 us)
Async XLA Ops:
  7.2 117.4 %copy-start = (bf16[512,2048]{1,0:T(8,128)(2,1)S(1)}, bf16[512,2048]{1,0:T(8,128)(2,1)}, u32[]{:S(2)}) copy-start(bf16[512,2048]{1,0:T(8,128)(2,1)} %param.17) | copy-start | bytes 6291460
  7.2 2.9 copy-start.10
  7.2 2.9 copy-start.14
  7.2 9.3 %copy-start.15 = (s32[1,4]{1,0:T(1,128)S(1)}, s32[1,4]{1,0:T(1,128)}, u32[]{:S(2)}) copy-start(s32[1,4]{1,0:T(1,128)} %param.21) | copy-start | bytes 52
  7.2 9.5 %copy-start.12 = (bf16[512]{0:T(512)(128)(2,1)S(1)}, bf16[512]{0:T(512)(128)(2,1)}, u32[]{:S(2)}) copy-start(bf16[512]{0:T(512)(128)(2,1)} %param.16) | copy-start | bytes 3076
  7.2 9.5 %copy-start.11 = (bf16[2048]{0:T(1024)(128)(2,1)S(1)}, bf16[2048]{0:T(1024)(128)(2,1)}, u32[]{:S(2)}) copy-start(bf16[2048]{0:T(1024)(128)(2,1)} %param.13) | copy-start | bytes 12292
  7.2 22.5 %all-gather.5.cloned.1.call-start = ((), (), s32[]{:S(2)}) async-start(), calls=%async_computation.1 | async-start | bytes 6291456 | tf_op jit(solution)/shard_map/all_gather | solution.py:74
  8.0 41.2 %all-gather.11.cloned.1.call-start = ((), (), s32[]{:S(2)}) async-start(), calls=%async_computation.4 | async-start | bytes 6291456 | tf_op jit(solution)/shard_map/all_gather | solution.py:94
  8.7 109.8 %all-gather.7.cloned.1.call-start = ((), (), s32[]{:S(2)}) async-start(), calls=%async_computation.2 | async-start | bytes 2662400 | tf_op jit(solution)/shard_map/all_gather | solution.py:87
  9.5 182.0 %all-gather.9.cloned.1.call-start = ((), (), s32[]{:S(2)}) async-start(), calls=%async_computation.3 | async-start | bytes 6389760 | tf_op jit(solution)/shard_map/all_gather | solution.py:82
  10.0 279.9 %reduce-scatter.2.cloned.1.call-start = ((), (), s32[]{:S(2)}) async-start(), calls=%async_computation.5 | async-start | bytes 6291456 | tf_op jit(solution)/shard_map/reduce_scatter | solution.py:140
  49.2 2.9 copy-start.2
  124.6 2.4 copy-start.3
  127.0 1.5 copy-start.13
  191.4 10.2 %copy-start.6 = (bf16[16,1536]{1,0:T(8,128)(2,1)S(1)}, bf16[16,1536]{1,0:T(8,128)(2,1)}, u32[]{:S(2)}) copy-start(bf16[16,1536]{1,0:T(8,128)(2,1)} %get-tuple-element.10) | copy-start | bytes 147460
  191.4 10.2 %copy-start.7 = (bf16[16,1536]{1,0:T(8,128)(2,1)S(1)}, bf16[16,1536]{1,0:T(8,128)(2,1)}, u32[]{:S(2)}) copy-start(bf16[16,1536]{1,0:T(8,128)(2,1)} %get-tuple-element.11) | copy-start | bytes 147460
  191.4 10.2 %copy-start.8 = (bf16[16,1536]{1,0:T(8,128)(2,1)S(1)}, bf16[16,1536]{1,0:T(8,128)(2,1)}, u32[]{:S(2)}) copy-start(bf16[16,1536]{1,0:T(8,128)(2,1)} %get-tuple-element.12) | copy-start | bytes 147460
  191.4 10.2 %copy-start.9 = (bf16[16,1536]{1,0:T(8,128)(2,1)S(1)}, bf16[16,1536]{1,0:T(8,128)(2,1)}, u32[]{:S(2)}) copy-start(bf16[16,1536]{1,0:T(8,128)(2,1)} %get-tuple-element.13) | copy-start | bytes 147460
  205.3 6.7 %copy-start.5 = (f32[1024,32]{0,1:T(8,128)S(1)}, f32[1024,32]{0,1:T(8,128)}, u32[]{:S(2)}) copy-start(f32[1024,32]{0,1:T(8,128)} %get-tuple-element.17) | copy-start | bytes 393220
  275.0 1.2 copy-start.4
  276.3 18.2 %copy-start.1 = (bf16[512,2048]{1,0:T(8,128)(2,1)S(1)}, bf16[512,2048]{1,0:T(8,128)(2,1)}, u32[]{:S(2)}) copy-start(bf16[512,2048]{1,0:T(8,128)(2,1)} %param.17) | copy-start | bytes 6291460
Sparse Core Ops, SparseCore 0:
  9.7 20.0 all-gather.4
  31.4 17.6 all-gather.10
  52.1 66.3 all-gather.6
  121.1 70.3 all-gather.8
  275.2 14.6 reduce-scatter.1
where the time goes:
time: 301 us
  waiting for transfers between devices  166 us (55%)
  matrix products  85.1 us (28%)
  between operations  19.1 us (6%)
  local copies, waits for them, and re-layouts  16.7 us (6%)
  other arithmetic  13.9 us (5%)
    all_gather x1, waiting for transfers between devices, body(): lax.all_gather(kva_weight, 'wide', axis=0, tiled=True)  64.3 us
    all_gather x1, waiting for transfers between devices, body(): lax.all_gather(q_weight, 'wide', axis=0, tiled=True)  60.1 us
    sub x1, matrix products, body(): expo = jnp.exp(scores - top)  26.8 us
    all_gather x1, waiting for transfers between devices, body(): stored = lax.all_gather(adapter_down, 'narrow', axis=1, tiled=True)  16.3 us
    dot_general x1, matrix products, body(): jnp.einsum('qhd,kd->hqk', query_vectors[..., NOPE:], key_rope, preferred_...  13.4 us
    dot_general x1, matrix products, body(): jnp.einsum('hqk,khd->qhd', weights, values, preferred_element_type=jnp.fl...  12.7 us
    reduce_scatter x1, waiting for transfers between devices, body(): lax.psum_scatter(partial_out.astype(jnp.bfloat16), 'narrow', scatter_dime...  12.6 us
    dot_general x1, matrix products, body(): jnp.dot(normed, lax.all_gather(q_weight, 'wide', axis=0, tiled=True), pre...  10.1 us
  transfers between devices with their start and end apart: 5, of which 5 were waited for; matrix products, arithmetic and copies ran while one was open for 9% of the time, Pallas kernels for 0%

commit v1 on v0

--- a/solution.py
+++ b/solution.py
@@ -11,6 +11,11 @@
 EPS = 1e-06
 THETA = 50000.0
 ADAPTER_SCALE = 2.0
+
+
+def gather_from_all(value, axis, dim):
+    copies = jnp.concatenate([value] * lax.axis_size(axis), axis=dim)
+    return lax.all_to_all(copies, axis, dim, dim, tiled=True)
 
 
 def rms_scale(values, gain):
@@ -83,9 +88,7 @@
         preferred_element_type=jnp.float32,
     )
     kv_pre = jnp.dot(
-        normed,
-        lax.all_gather(kva_weight, "wide", axis=0, tiled=True),
-        preferred_element_type=jnp.float32,
+        normed, gather_from_all(kva_weight, "wide", 0), preferred_element_type=jnp.float32
     )
     prompt_ids = adapter_ids[0]
     id_hot = (prompt_ids[:, None] == jnp.arange(adapter_slot.shape[0])[None, :]).astype(jnp.int32)

time: 301 us -> 235 us (0.78)
  waiting for transfers between devices: 166 us -> 80.2 us
  starting transfers between devices: 0.19 us -> 12.5 us
  local copies, waits for them, and re-layouts: 16.7 us -> 21.9 us
    all_gather x1 -> x0, waiting for transfers between devices: 64.3 us -> none  [body(): lax.all_gather(kva_weight, 'wide', axis=0, tiled=True)]
    all_to_all x0 -> x1, waiting for transfers between devices: none -> 20.6 us  [gather_from_all(): return lax.all_to_all(copies, axis, dim, dim, tiled=True)]
    all_gather x1, waiting for transfers between devices: 16.3 us -> 0.01 us  [body(): stored = lax.all_gather(adapter_down, 'narrow', axis=1, tiled=True)]
    all_gather x1, waiting for transfers between devices: 60.1 us -> 44.9 us  [body(): lax.all_gather(q_weight, 'wide', axis=0, tiled=True)]
    all_to_all x0 -> x1, starting transfers between devices: none -> 12.3 us  [gather_from_all(): return lax.all_to_all(copies, axis, dim, dim, tiled=True)]
    all_gather x1, waiting for transfers between devices: 10.1 us -> 0.02 us  [body(): whole = lax.all_gather(tokens, 'narrow', axis=1, tiled=True)]
    unnamed x33 -> x104, local copies, waits for them, and re-layouts: 3.27 us -> 8.41 us
  transfers between devices with their start and end apart: 5 -> 5, of which waited for: 5 -> 3; matrix products, arithmetic and copies ran while one was open for 9% -> 13% of each run, Pallas kernels for 0% -> 0%
where the time goes in v1:
time: 235 us; the launch traced here: 234 us
  matrix products  85.1 us (36%)
  waiting for transfers between devices  80.2 us (34%)
  local copies, waits for them, and re-layouts  21.9 us (9%)
  between operations  19.5 us (8%)
  other arithmetic  14.8 us (6%)
  starting transfers between devices  12.5 us (5%)
    all_gather x1, waiting for transfers between devices, body(): lax.all_gather(q_weight, 'wide', axis=0, tiled=True)  44.9 us
    sub x1, matrix products, body(): expo = jnp.exp(scores - top)  26.8 us
    all_to_all x1, waiting for transfers between devices, gather_from_all(): return lax.all_to_all(copies, axis, dim, dim, tiled=True)  20.6 us
    dot_general x1, matrix products, body(): jnp.einsum('qhd,kd->hqk', query_vectors[..., NOPE:], key_rope, preferred_...  13.2 us
    dot_general x1, matrix products, body(): jnp.einsum('hqk,khd->qhd', weights, values, preferred_element_type=jnp.fl...  12.7 us
    reduce_scatter x1, waiting for transfers between devices, body(): lax.psum_scatter(partial_out.astype(jnp.bfloat16), 'narrow', scatter_dime...  12.5 us
    all_to_all x1, starting transfers between devices, gather_from_all(): return lax.all_to_all(copies, axis, dim, dim, tiled=True)  12.3 us
    dot_general x1, matrix products, body(): jnp.dot(normed, lax.all_gather(q_weight, 'wide', axis=0, tiled=True), pre...  10.4 us
  transfers between devices with their start and end apart: 5, of which 3 were waited for; matrix products, arithmetic and copies ran while one was open for 13% of the time, Pallas kernels for 0%

profile of v1, /device:TPU:1, one launch (start us, length us, event | category | flops | bytes accessed | tf_op | source)
XLA Modules:
  0.0 234.1 jit_solution(6093972369936686567)
XLA Ops:
  7.2 0.0 copy-start
  7.2 0.0 all-gather.4.cloned.1.call-start
  7.2 0.7 all-gather.4.cloned.1.call-update
  7.9 0.0 all-gather.8.cloned.1.call-start
  8.0 0.7 all-gather.8.cloned.1.call-update
  8.7 0.0 all-gather.6.cloned.1.call-start
  8.7 0.7 all-gather.6.cloned.1.call-update
  10.4 1.5 copy-done.8
  11.9 0.0 copy-start.15
  11.9 12.3 %all-to-all-start = ((bf16[64,32,576]{2,1,0:T(8,128)(2,1)}), bf16[64,32,576]{2,1,0:T(8,128)(2,1)}, u32[]{:S(2)}, u32[]{:S(2)}) async-start(bf16[64,32,576]{2,1,0:T(8,128)(2,1)} %bitcast.49), calls=%async_computation | async-start | bytes 5242880 | tf_op jit(solution)/shard_map/all_to_all | solution.py:18
  24.3 0.0 reduce-scatter.2.cloned.1.call-start
  24.3 0.2 select_reduce_fusion.1
  24.5 0.7 fusion.47
  27.8 0.7 fusion.46
  31.1 0.2 reduce-window.4
  31.4 0.5 multiply_exponential_fusion
  31.9 0.1 convert_reduce_fusion
  32.0 0.1 select_reduce_fusion
  32.1 1.6 constant_dynamic-slice_fusion.3
  33.7 0.6 fusion.7
  34.3 0.0 all-gather.4.cloned.1.call-done
  34.3 3.1 %fusion.4 = f32[1024]{0:T(1024)S(1)} fusion(bf16[1024,2048]{1,0:T(8,128)(2,1)} %all-gather.4.cloned.1.call-done), kind=kLoop, calls=%fused_computation.9 | loop fusion | flops 6290432 | bytes 4198400 | tf_op jit(solution)/shard_map/reduce_sum | solution.py:22
  37.4 20.6 %all-to-all-done = bf16[64,32,576]{2,1,0:T(8,128)(2,1)} async-done(((bf16[64,32,576]{2,1,0:T(8,128)(2,1)}), bf16[64,32,576]{2,1,0:T(8,128)(2,1)}, u32[]{:S(2)}, u32[]{:S(2)}) %all-to-all-start) | async-done | bytes 2359328 | tf_op jit(solution)/shard_map/all_to_all | solution.py:18
  58.0 5.7 %fusion.43 = f32[1024,576]{0,1:T(8,128)S(1)} fusion(bf16[2048,576]{1,0:T(8,128)(2,1)} %bitcast.1, bf16[1024,2048]{1,0:T(8,128)(2,1)} %all-gather.4.cloned.1.call-done, f32[2048]{0:T(1024)S(1)} %convert_element_type.88, f32[1024]{0:T(1024)S(1)} %add_rsqrt_fusion.1), kind=kOutput, calls=%fused_computation.145 | convolution fusion | flops 2424307712 | bytes 8925184 | tf_op jit(solution)/shard_map/dot_general | solution.py:90
  63.7 0.2 multiply_reduce_fusion
  63.9 0.2 multiply_convert_fusion
  64.2 0.9 copy-done.4
  65.1 2.4 %convolution_convert_fusion = bf16[1024,2048]{1,0:T(8,128)(2,1)S(1)} fusion(bf16[1024,512]{0,1:T(8,128)(2,1)S(1)} %multiply_convert_fusion, bf16[512,2048]{1,0:T(8,128)(2,1)S(1)} %copy-done), kind=kOutput, calls=%fused_computation.17 | convolution fusion | flops 2149580800 | bytes 7340032 | tf_op jit(solution)/shard_map/dot_general | solution.py:121
  67.5 3.4 %copy.40 = bf16[128,8,8,256]{3,2,1,0:T(8,128)(2,1)} copy(bf16[128,8,8,256]{3,1,2,0:T(8,128)(2,1)S(1)} %bitcast.48) | data formatting | bytes 8388608
  70.9 2.4 %constant_dynamic-slice_fusion.7 = (bf16[2048,16]{1,0:T(8,128)(2,1)S(1)}, bf16[2048,16]{1,0:T(8,128)(2,1)S(1)}, bf16[2048,16]{1,0:T(8,128)(2,1)S(1)}, bf16[2048,16]{1,0:T(8,128)(2,1)S(1)}) fusion(bf16[2048,1024]{1,0:T(8,128)(2,1)} %all-gather.8.cloned.1.call-done, s32[]{:T(128)S(6)} %select_n.28, s32[]{:T(128)S(6)} %select_n.31, s32[]{:T(128)S(6)} %select_n.30, ...), kind=kLoop, calls=%fused_computation.137 | loop fusion | bytes 524304 | tf_op jit(solution)/shard_map/dynamic_slice | solution.py:56
  73.3 0.6 copy-done.5
  73.9 2.0 fusion.17
  76.0 2.2 subtract_convert_fusion.1
  78.1 1.6 fusion.45
  79.7 44.9 %all-gather.6.cloned.1.call-done = bf16[2048,1536]{1,0:T(8,128)(2,1)} async-done(((bf16[32,1536]{1,0:T(8,128)(2,1)}), bf16[2048,1536]{1,0:T(8,128)(2,1)}) %all-gather.6.cloned.1.call-update) | async-done | bytes 6291472 | tf_op jit(solution)/shard_map/all_gather | solution.py:87
  124.7 10.4 %fusion.41 = f32[1024,1536]{1,0:T(8,128)S(1)} fusion(bf16[2048,1536]{1,0:T(8,128)(2,1)} %all-gather.6.cloned.1.call-done, bf16[1024,2048]{1,0:T(8,128)(2,1)} %all-gather.4.cloned.1.call-done, f32[2048]{0:T(1024)S(1)} %convert_element_type.88, f32[1024]{0:T(1024)S(1)} %add_rsqrt_fusion.1), kind=kOutput, calls=%fused_computation.144 | convolution fusion | flops 6450839552 | bytes 16789504 | tf_op jit(solution)/shard_map/dot_general | solution.py:85
  135.1 3.7 %multiply_add_fusion = f32[1024,1536]{1,0:T(8,128)} fusion(f32[1024,1536]{1,0:T(8,128)S(1)} %fusion.41, bf16[1024,64]{0,1:T(8,128)(2,1)S(1)} %bitcast.50, bf16[16,1536]{1,0:T(8,128)(2,1)S(1)} %copy-done.12, bf16[16,1536]{1,0:T(8,128)(2,1)S(1)} %copy-done.13, bf16[16,1536]{1,0:T(8,128)(2,1)S(1)} %copy-done.11, bf16[16,1536]{1,0:T(8,128)(2,1)S(1)} %copy-done.10), kind=kOutput, calls=%fused_computation.12 | convolution fusion | flops 205258752 | bytes 12910592 | tf_op jit(solution)/shard_map/dot_general | solution.py:111
  138.8 6.6 %copy.32 = f32[1024,1536]{0,1:T(8,128)} copy(f32[1024,1536]{1,0:T(8,128)} %multiply_add_fusion) | data formatting | bytes 12582912 | tf_op jit(solution)/shard_map/add | solution.py:111
  145.4 1.9 subtract_convert_fusion
  147.3 13.2 %fusion.13 = f32[1024,1024,8]{1,0,2:T(8,128)} fusion(bf16[1024,8,32]{0,2,1:T(8,128)(2,1)S(1)} %get-tuple-element.3, bf16[1024,8,32]{0,2,1:T(8,128)(2,1)S(1)} %get-tuple-element.2, bf16[1024,32]{0,1:T(8,128)(2,1)S(1)} %get-tuple-element.15, bf16[1024,32]{0,1:T(8,128)(2,1)S(1)} %get-tuple-element.14), kind=kOutput, calls=%fused_computation.25 | convolution fusion | flops 1076101120 | bytes 34734080 | tf_op jit(solution)/shard_map/qhd,kd->hqk/dot_general | solution.py:129
  160.5 26.8 %fusion.48 = (f32[8,1024]{1,0:T(8,128)S(1)}, f32[8,1024,1024]{1,2,0:T(8,128)}) fusion(f32[1024,1024,8]{1,0,2:T(8,128)} %fusion.13, pred[1024,1024]{0,1:T(8,128)(4,1)S(1)} %fusion.7, f32[1024,8,192]{0,2,1:T(8,128)} %bitcast.46, bf16[1024,8,128]{2,1,0:T(8,128)(2,1)S(1)} %get-tuple-element.5), kind=kOutput, calls=%fused_computation.149 | convolution fusion | flops 2189427712 | bytes 72384512 | tf_op jit(solution)/shard_map/sub | solution.py:136
  187.2 12.7 %fusion.10 = bf16[8,128,1024]{2,1,0:T(8,128)(2,1)S(1)} fusion(f32[8,1024,1024]{1,2,0:T(8,128)} %get-tuple-element.29, f32[8,1024]{1,0:T(8,128)S(1)} %get-tuple-element.28, bf16[1024,8,128]{2,1,0:T(8,128)(2,1)} %get-tuple-element.4), kind=kOutput, calls=%fused_computation.23 | convolution fusion | flops 2165309440 | bytes 37781504 | tf_op jit(solution)/shard_map/hqk,khd->qhd/dot_general | solution.py:138
  199.9 8.3 %convolution_convert_fusion.1 = bf16[1024,2048]{1,0:T(8,128)(2,1)} fusion(bf16[1024,1024]{0,1:T(8,128)(2,1)S(1)} %bitcast.55, bf16[1024,2048]{1,0:T(8,128)(2,1)} %param.18), kind=kOutput, calls=%fused_computation.18 | convolution fusion | flops 4297064448 | bytes 10485760 | tf_op jit(solution)/shard_map/dot_general | solution.py:142
  208.3 0.0 reduce-scatter.2.cloned.1.call-update
  208.3 1.2 copy-done.7
  209.5 1.1 pad_maximum_fusion
  210.6 12.5 %reduce-scatter.2.cloned.1.call-done = bf16[1024,1024]{1,0:T(8,128)(2,1)} async-done(((bf16[1024,2048]{1,0:T(8,128)(2,1)}), bf16[1024,1024]{1,0:T(8,128)(2,1)}) %reduce-scatter.2.cloned.1.call-update) | async-done | bytes 2097168 | tf_op jit(solution)/shard_map/reduce_scatter | solution.py:143
  223.1 4.5 %add_convert_fusion = bf16[1024,1024]{1,0:T(8,128)(2,1)} fusion(bf16[1024,1024]{1,0:T(8,128)(2,1)} %reduce-scatter.2.cloned.1.call-done, bf16[1024,1024]{1,0:T(8,128)(2,1)} %param.12), kind=kLoop, calls=%fused_computation.14 | loop fusion | flops 4194304 | bytes 6291456 | tf_op jit(solution)/shard_map/convert_element_type | solution.py:146
  (108 shorter events, 0.9 us)
Async XLA Ops:
  7.2 57.9 %copy-start = (bf16[512,2048]{1,0:T(8,128)(2,1)S(1)}, bf16[512,2048]{1,0:T(8,128)(2,1)}, u32[]{:S(2)}) copy-start(bf16[512,2048]{1,0:T(8,128)(2,1)} %param.17) | copy-start | bytes 6291460
  7.2 2.2 copy-start.2
  7.2 27.1 %all-gather.4.cloned.1.call-start = ((), (), s32[]{:S(2)}) async-start(), calls=%async_computation.2 | async-start | bytes 6291456 | tf_op jit(solution)/shard_map/all_gather | solution.py:79
  7.9 63.0 %all-gather.8.cloned.1.call-start = ((), (), s32[]{:S(2)}) async-start(), calls=%async_computation.4 | async-start | bytes 6291456 | tf_op jit(solution)/shard_map/all_gather | solution.py:97
  8.7 116.0 %all-gather.6.cloned.1.call-start = ((), (), s32[]{:S(2)}) async-start(), calls=%async_computation.3 | async-start | bytes 6389760 | tf_op jit(solution)/shard_map/all_gather | solution.py:87
  10.4 1.5 copy-start.8
  11.9 12.4 %copy-start.14 = (s32[1,4]{1,0:T(1,128)S(1)}, s32[1,4]{1,0:T(1,128)}, u32[]{:S(2)}) copy-start(s32[1,4]{1,0:T(1,128)} %param.22) | copy-start | bytes 52
  11.9 12.4 %copy-start.18 = (s32[64]{0:T(128)S(1)}, s32[64]{0:T(128)}, u32[]{:S(2)}) copy-start(s32[64]{0:T(128)} %param.23) | copy-start | bytes 772
  11.9 19.2 %copy-start.19 = (s32[1,4]{1,0:T(1,128)S(1)}, s32[1,4]{1,0:T(1,128)}, u32[]{:S(2)}) copy-start(s32[1,4]{1,0:T(1,128)} %param.21) | copy-start | bytes 52
  11.9 19.4 %copy-start.16 = (bf16[512]{0:T(512)(128)(2,1)S(1)}, bf16[512]{0:T(512)(128)(2,1)}, u32[]{:S(2)}) copy-start(bf16[512]{0:T(512)(128)(2,1)} %param.16) | copy-start | bytes 3076
  11.9 19.4 %copy-start.15 = (bf16[2048]{0:T(1024)(128)(2,1)S(1)}, bf16[2048]{0:T(1024)(128)(2,1)}, u32[]{:S(2)}) copy-start(bf16[2048]{0:T(1024)(128)(2,1)} %param.13) | copy-start | bytes 12292
  11.9 46.1 %all-to-all-start = ((bf16[64,32,576]{2,1,0:T(8,128)(2,1)}), bf16[64,32,576]{2,1,0:T(8,128)(2,1)}, u32[]{:S(2)}, u32[]{:S(2)}) async-start(bf16[64,32,576]{2,1,0:T(8,128)(2,1)} %bitcast.49), calls=%async_computation | async-start | bytes 5242880 | tf_op jit(solution)/shard_map/all_to_all | solution.py:18
  24.3 198.8 %reduce-scatter.2.cloned.1.call-start = ((), (), s32[]{:S(2)}) async-start(), calls=%async_computation.5 | async-start | bytes 6291456 | tf_op jit(solution)/shard_map/reduce_scatter | solution.py:143
  63.7 1.4 copy-start.4
  65.1 2.4 %copy-start.6 = (bf16[1024,512]{0,1:T(8,128)(2,1)}, bf16[1024,512]{0,1:T(8,128)(2,1)S(1)}, u32[]{:S(2)}) copy-start(bf16[1024,512]{0,1:T(8,128)(2,1)S(1)} %multiply_convert_fusion) | copy-start | bytes 3145732
  70.9 2.9 %copy-start.5 = (bf16[1024,2048]{1,0:T(8,128)(2,1)S(1)}, bf16[1024,2048]{1,0:T(8,128)(2,1)}, u32[]{:S(2)}) copy-start(bf16[1024,2048]{1,0:T(8,128)(2,1)} %all-gather.4.cloned.1.call-done) | copy-start | bytes 12582916
  73.8 2.1 copy-start.17
  73.9 4.3 %copy-start.3 = (bf16[128,8,8,256]{3,2,1,0:T(8,128)(2,1)S(1)}, bf16[128,8,8,256]{3,2,1,0:T(8,128)(2,1)}, u32[]{:S(2)}) copy-start(bf16[128,8,8,256]{3,2,1,0:T(8,128)(2,1)} %copy.40) | copy-start | bytes 12582916
  124.7 10.4 %copy-start.10 = (bf16[16,1536]{1,0:T(8,128)(2,1)S(1)}, bf16[16,1536]{1,0:T(8,128)(2,1)}, u32[]{:S(2)}) copy-start(bf16[16,1536]{1,0:T(8,128)(2,1)} %get-tuple-element.10) | copy-start | bytes 147460
  124.7 10.4 %copy-start.11 = (bf16[16,1536]{1,0:T(8,128)(2,1)S(1)}, bf16[16,1536]{1,0:T(8,128)(2,1)}, u32[]{:S(2)}) copy-start(bf16[16,1536]{1,0:T(8,128)(2,1)} %get-tuple-element.11) | copy-start | bytes 147460
  124.7 10.4 %copy-start.12 = (bf16[16,1536]{1,0:T(8,128)(2,1)S(1)}, bf16[16,1536]{1,0:T(8,128)(2,1)}, u32[]{:S(2)}) copy-start(bf16[16,1536]{1,0:T(8,128)(2,1)} %get-tuple-element.12) | copy-start | bytes 147460
  124.7 10.4 %copy-start.13 = (bf16[16,1536]{1,0:T(8,128)(2,1)S(1)}, bf16[16,1536]{1,0:T(8,128)(2,1)}, u32[]{:S(2)}) copy-start(bf16[16,1536]{1,0:T(8,128)(2,1)} %get-tuple-element.13) | copy-start | bytes 147460
  138.8 6.7 %copy-start.9 = (f32[1024,32]{0,1:T(8,128)S(1)}, f32[1024,32]{0,1:T(8,128)}, u32[]{:S(2)}) copy-start(f32[1024,32]{0,1:T(8,128)} %get-tuple-element.17) | copy-start | bytes 393220
  208.3 1.2 copy-start.7
  209.5 18.1 %copy-start.1 = (bf16[512,2048]{1,0:T(8,128)(2,1)S(1)}, bf16[512,2048]{1,0:T(8,128)(2,1)}, u32[]{:S(2)}) copy-start(bf16[512,2048]{1,0:T(8,128)(2,1)} %param.17) | copy-start | bytes 6291460
Sparse Core Ops, SparseCore 0:
  9.7 20.0 all-gather.3
  31.4 17.6 all-gather.7
  51.9 72.7 all-gather.5
  208.4 14.6 reduce-scatter.1
